TPU v7x, 32 devices: a whole 2x2x4 slice. The times are simulated.
32 devices in a mesh: exp: 4 (over z), row: 4 (over y, core), col: 2 (over x).
Axes of the slice: x: 2, y: 2, z: 4, core: 2. Of those that a mesh axis runs over, the one named last changes fastest.
Arguments:
- exposures: float32 [64, 128, 1024], P('exp', 'row', 'col'), may hold values from -6 to 6
- bad_pixels: int32 [64, 128, 1024], P('exp', 'row', 'col'), may hold values 0 or 1
- offsets: int32 [64, 2], P('exp'), may hold values from -8 to 8, as said below
- warp_index: int32 [64, 2], P('exp'), may hold values from 0 to 15
- blur_index: int32 [64], P('exp'), may hold values from 0 to 7
Outputs:
- residual: float32 [64, 128, 1024], P('exp', 'row', 'col')
- median_sky: float32 [128, 1024], P('row', 'col')
Inputs may be any that keep to these rules, and one draw needn't show every extreme that they name: `offsets`: in each component some exposure has the offset -8 and some has 8.
All inputs are finite; a program needn't handle non-finite values. No bound on the sum of `bad_pixels` on one device may be relied on, other than what follows from the above.
Results may differ from a plain program's by a relative error of at most 0.0003.
Values sent between devices are 32-bit elements; how exact they have to be, the bound alone decides.
No kernel may reach another device: no remote copies, remote signals or barrier semaphores. Data moves between devices by JAX's collectives and lax.ppermute only.
A program may use at most 64 MiB of HBM per device.

v0:
```python
import jax
import jax.numpy as jnp
from jax import lax
from jax.sharding import PartitionSpec as P

NFRAC = 16
NPSF = 8
PSF_RADIUS = 4
PASSES = 16
HALO = 11
sentinel = 1000000.0
half_sentinel = 500000.0
pivot_span = 16.0


def _row_halo(block, dim, width):
    count = lax.axis_size("row")
    forward = [(i, i + 1) for i in range(count - 1)]
    backward = [(target, source) for source, target in forward]
    size = block.shape[dim]
    low = lax.ppermute(lax.slice_in_dim(block, size - width, None, axis=dim), "row", forward)
    high = lax.ppermute(lax.slice_in_dim(block, 0, width, axis=dim), "row", backward)
    return jnp.concatenate([low, block, high], axis=dim)


def _col_halo(block, dim, width):
    count = lax.axis_size("col")
    size = block.shape[dim]
    right_edge = lax.slice_in_dim(block, size - width, None, axis=dim)
    left_edge = lax.slice_in_dim(block, 0, width, axis=dim)
    if count != 2:
        forward = [(i, i + 1) for i in range(count - 1)]
        backward = [(target, source) for source, target in forward]
        low = lax.ppermute(right_edge, "col", forward)
        high = lax.ppermute(left_edge, "col", backward)
        return jnp.concatenate([low, block, high], axis=dim)
    first = lax.axis_index("col") == 0
    outgoing = jnp.moveaxis(jnp.where(first, right_edge, left_edge), dim, 0)
    packed_shape = outgoing.shape
    packed = outgoing.reshape(width, -1)
    arrived = lax.ppermute(packed, "col", [(0, 1), (1, 0)])
    arrived = jnp.moveaxis(arrived.reshape(packed_shape), 0, dim)
    zeros = jnp.zeros_like(arrived)
    low = jnp.where(first, zeros, arrived)
    high = jnp.where(first, arrived, zeros)
    return jnp.concatenate([low, block, high], axis=dim)


def extended(block, row_dim, col_dim, width):
    return _col_halo(_row_halo(block, row_dim, width), col_dim, width)


def lanczos_table():
    fraction = jnp.arange(NFRAC, dtype=jnp.float32) / NFRAC
    offset_grid = jnp.arange(-2, 4, dtype=jnp.float32)
    spread = offset_grid[None, :] - fraction[:, None]
    kernel = jnp.sinc(spread) * jnp.sinc(spread / 3.0)
    return kernel / jnp.sum(kernel, axis=1, keepdims=True)


def blur_table():
    offset_grid = jnp.arange(-PSF_RADIUS, PSF_RADIUS + 1, dtype=jnp.float32)
    widths = 0.7 + 0.2 * jnp.arange(NPSF, dtype=jnp.float32)
    kernel = jnp.exp(-0.5 * (offset_grid[None, :] / widths[:, None]) ** 2)
    return kernel / jnp.sum(kernel, axis=1, keepdims=True)


def lookup(indices, entries, kernel_table):
    chooser = (indices[:, None] == lax.broadcasted_iota(jnp.int32, (1, entries), 1)).astype(
        jnp.float32
    )
    return jnp.dot(chooser, kernel_table, precision=lax.Precision.HIGHEST)


def placed_taps(weights, shifts):
    reach = 2 * HALO + 1
    positions = lax.broadcasted_iota(jnp.int32, (1, 1, reach), 2)
    tap_slot = HALO + shifts[:, None, None] + lax.broadcasted_iota(jnp.int32, (1, 6, 1), 1) - 2
    spread = (tap_slot == positions).astype(jnp.float32)
    return jnp.sum(weights[:, :, None] * spread, axis=1)


def resample_axis(stack, coefficients, out_len, which_axis):
    out_shape = list(stack.shape)
    out_shape[which_axis] = out_len
    total = jnp.zeros(tuple(out_shape), jnp.float32)
    for position in range(2 * HALO + 1):
        window = lax.slice_in_dim(stack, position, position + out_len, 1, which_axis)
        total = total + coefficients[:, position, None, None] * window
    return total


def bisect_lower(valid_count, count_below):

    def one_pass(sweep_no, bounds):
        lower_edge, upper_edge = bounds
        middle = 0.5 * (lower_edge + upper_edge)
        enough = 2.0 * count_below(middle) >= valid_count
        return (jnp.where(enough, lower_edge, middle), jnp.where(enough, middle, upper_edge))

    initial = (
        jnp.full(valid_count.shape, -pivot_span, jnp.float32),
        jnp.full(valid_count.shape, pivot_span, jnp.float32),
    )
    return lax.fori_loop(0, PASSES, one_pass, initial)[0]


def stack_median(pixel_stack):
    valid_count = jnp.sum(pixel_stack < half_sentinel, axis=0, dtype=jnp.float32)

    def count_below(middle):
        return jnp.sum(pixel_stack <= middle[None], axis=0, dtype=jnp.float32)

    lower_edge = bisect_lower(valid_count, count_below)
    return jnp.min(jnp.where(pixel_stack > lower_edge[None], pixel_stack, sentinel), axis=0)


def body(exposures, bad_pixels, offsets, warp_index, blur_index):
    group_size, row_count, col_count = exposures.shape
    kernel_table = lanczos_table()
    coef_down = placed_taps(lookup(warp_index[:, 0], NFRAC, kernel_table), offsets[:, 0])
    coef_across = placed_taps(lookup(warp_index[:, 1], NFRAC, kernel_table), offsets[:, 1])
    padded = extended(exposures, 1, 2, HALO)
    across = resample_axis(padded, coef_down, row_count, 1)
    warped = resample_axis(across, coef_across, col_count, 2)
    flagged = jnp.where(bad_pixels == 1, sentinel, warped)
    band = stack_median(lax.all_to_all(flagged, "exp", split_axis=1, concat_axis=0, tiled=True))
    groups = lax.axis_size("exp")
    median_sky = lax.all_to_all(
        jnp.tile(band, (groups, 1)), "exp", split_axis=0, concat_axis=0, tiled=True
    )
    bordered = extended(median_sky, 0, 1, PSF_RADIUS)
    blur = blur_table()
    taps = 2 * PSF_RADIUS + 1
    blurred_rows = jnp.zeros((NPSF, row_count, col_count + 2 * PSF_RADIUS), jnp.float32)
    for tap_no in range(taps):
        blurred_rows = (
            blurred_rows
            + blur[:, tap_no, None, None] * bordered[None, tap_no : tap_no + row_count, :]
        )
    smoothed = jnp.zeros((NPSF, row_count, col_count), jnp.float32)
    for tap_no in range(taps):
        smoothed = (
            smoothed + blur[:, tap_no, None, None] * blurred_rows[:, :, tap_no : tap_no + col_count]
        )
    chooser = (blur_index[:, None] == lax.broadcasted_iota(jnp.int32, (1, NPSF), 1)).astype(
        jnp.float32
    )
    sky_model = jnp.zeros((group_size, row_count, col_count), jnp.float32)
    for kernel_no in range(NPSF):
        sky_model = sky_model + chooser[:, kernel_no, None, None] * smoothed[kernel_no][None]
    residual = jnp.where(bad_pixels == 1, 0.0, warped - sky_model)
    return (residual, median_sky)


def solution(mesh):
    return jax.shard_map(
        body,
        mesh=mesh,
        in_specs=(
            P("exp", "row", "col"),
            P("exp", "row", "col"),
            P("exp", None),
            P("exp", None),
            P("exp"),
        ),
        out_specs=(P("exp", "row", "col"), P("row", "col")),
        check_vma=False,
    )
```

profile of v0, /device:TPU:0, one launch (start us, length us, event | category | flops | bytes accessed | tf_op | source)
XLA Modules:
  0.0 90.9 jit_solution(72379477720639308)
XLA Ops:
  0.6 1.3 %fusion.134 = (f32[16,11,512]{2,1,0:T(8,128)S(1)}, f32[16,11,512]{2,1,0:T(8,128)S(1)}) fusion(f32[16,32,512]{2,1,0:T(8,128)} %param.8), kind=kLoop, calls=%fused_computation.315 | loop fusion | bytes 1441792 | tf_op jit(solution)/shard_map/slice | solution.py:22
  2.2 3.3 %collective-permute-start = (f32[16,11,512]{2,0,1:T(8,128)S(1)}, f32[16,11,512]{2,0,1:T(8,128)}, u32[]{:S(2)}, u32[]{:S(2)}) collective-permute-start(f32[16,11,512]{2,0,1:T(8,128)S(1)} %copy.47), channel_id=1, source_target_pairs={{0,2},{2,4},{4,6},{1,3},{3,5},{5,7},{8,10},{10,12},{12,14},{9,11},... | collective-permute-start | bytes 1081352 | tf_op jit(solution)/shard_map/ppermute | solution.py:21
  5.7 1.3 %collective-permute-start.1 = (f32[16,11,512]{2,0,1:T(8,128)S(1)}, f32[16,11,512]{2,0,1:T(8,128)S(1)}, u32[]{:S(2)}, u32[]{:S(2)}) collective-permute-start(f32[16,11,512]{2,0,1:T(8,128)S(1)} %copy.48), channel_id=1, source_target_pairs={{2,0},{4,2},{6,4},{3,1},{5,3},{7,5},{10,8},{12,10},{14,12},{11,9},... | collective-permute-start | bytes 1081352 | tf_op jit(solution)/shard_map/ppermute | solution.py:22
  7.7 0.8 slice_reduce_fusion.43
  8.5 1.1 %slice_reduce_fusion.44 = (f32[16]{0:T(128)}, f32[16]{0:T(128)}, f32[16]{0:T(128)}, f32[16]{0:T(128)}, f32[16]{0:T(128)}, /*index=5*/f32[16]{0:T(128)}, f32[16]{...) fusion(f32[16,23]{1,0:T(8,128)S(1)} %select_reduce_fusion), kind=kLoop, calls=%fused_computation.204 | loop fusion | bytes 2432 | tf_op jit(solution)/shard_map/slice | solution.py:89
  9.7 1.1 %slice_reduce_fusion.45 = (f32[16]{0:T(128)S(1)}, f32[16]{0:T(128)S(1)}, f32[16]{0:T(128)}, f32[16]{0:T(128)}, f32[16]{0:T(128)}, /*index=5*/f32[16]{0:T(128)}, ...) fusion(f32[16,23]{1,0:T(8,128)S(1)} %select_reduce_fusion.1), kind=kLoop, calls=%fused_computation.205 | loop fusion | bytes 2432 | tf_op jit(solution)/shard_map/slice | solution.py:89
  10.7 1.0 %constant_dynamic-update-slice_fusion.2 = f32[16,54,512]{2,0,1:T(8,128)S(1)} fusion(f32[16,11,512]{2,0,1:T(8,128)} %collective-permute-done), kind=kLoop, calls=%fused_computation.208 | loop fusion | bytes 720896
  11.8 0.6 constant_dynamic-update-slice_fusion.1
  13.0 2.4 %collective-permute-start.2 = (f32[11,864]{1,0:T(8,128)S(1)}, f32[11,864]{1,0:T(8,128)S(1)}, u32[]{:S(2)}, u32[]{:S(2)}) collective-permute-start(f32[11,864]{1,0:T(8,128)S(1)} %reshape.187), channel_id=1, source_target_pairs={{0,1},{1,0},{2,3},{3,2},{4,5},{5,4},{6,7},{7,6},{8,9},{9,8},{10,11... | collective-permute-start | bytes 114056 | tf_op jit(solution)/shard_map/ppermute | solution.py:41
  15.6 1.9 %collective-permute-done.2 = f32[11,864]{1,0:T(8,128)S(1)} collective-permute-done((f32[11,864]{1,0:T(8,128)S(1)}, f32[11,864]{1,0:T(8,128)S(1)}, u32[]{:S(2)}, u32[]{:S(2)}) %collective-permute-start.2) | collective-permute-done | bytes 38048 | tf_op jit(solution)/shard_map/ppermute | solution.py:41
  17.6 0.3 copy.42
  18.1 0.3 copy.41
  18.6 0.7 pad_maximum_fusion
  19.8 3.9 %fusion = f32[16,32,534]{2,0,1:T(8,128)S(1)} fusion(f32[16,54,534]{2,0,1:T(8,128)S(1)} %pad_maximum_fusion, f32[16]{0:T(128)S(1)} %copy-done.24, f32[16]{0:T(128)S(1)} %copy-done.25, f32[16]{0:T(128)S(1)} %copy-done.26, f32[16]{0:T(128)S(1)} %copy-done.27, f32[16]{0:T(128)S(1)} %copy-done.28, f32[16]{0:T(128)S(1)} %copy-done.29, f32[16]{0:T(128)S(1)} %copy-done.30, ...), kind=kLoop, calls=%fused_computation.8 | loop fusion | flops 12303360 | bytes 26248640 | tf_op jit(solution)/shard_map/add | solution.py:89
  23.8 7.0 %broadcast_select_fusion = (f32[16,32,512]{2,0,1:T(8,128)}, f32[16,32,512]{2,0,1:T(8,128)S(1)}, pred[16,32,512]{2,0,1:T(8,128)(4,1)S(1)}) fusion(f32[16,32,534]{2,0,1:T(8,128)S(1)} %fusion, f32[16]{0:T(128)S(1)} %get-tuple-element.56, f32[16]{0:T(128)S(1)} %copy-done.2, f32[16]{0:T(128)S(1)} %copy-done.3, f32[16]{0:T(128)S(1)} %copy-done.4, ...), kind=kLoop, calls=%fused_computation.119 | loop fusion | flops 12320768 | bytes 27526592 | tf_op jit(solution)/shard_map/jit(_where)/select_n | solution.py:126
  30.8 5.4 %all-to-all-start = ((f32[16,32,512]{2,0,1:T(8,128)}), f32[16,32,512]{2,0,1:T(8,128)S(1)}, u32[]{:S(2)}, u32[]{:S(2)}) async-start(f32[16,32,512]{2,0,1:T(8,128)} %get-tuple-element.113), calls=%async_computation | async-start | bytes 2097152 | tf_op jit(solution)/shard_map/all_to_all | solution.py:127
  36.4 26.2 %all-to-all-done = f32[16,32,512]{2,0,1:T(8,128)S(1)} async-done(((f32[16,32,512]{2,0,1:T(8,128)}), f32[16,32,512]{2,0,1:T(8,128)S(1)}, u32[]{:S(2)}, u32[]{:S(2)}) %all-to-all-start) | async-done | bytes 1048608 | tf_op jit(solution)/shard_map/all_to_all | solution.py:127
  62.6 0.6 copy.43
  63.4 3.6 %while.13 = (s32[]{:T(128)}, f32[8,512]{1,0:T(8,128)S(1)}, f32[8,512]{1,0:T(8,128)S(1)}, f32[64,8,512]{2,1,0:T(8,128)S(1)}, f32[8,512]{1,0:T(8,128)S(1)}, /*index=5*/s32[]{:T(128)}, s32[]{:T(128)}) while((s32[]{:T(128)}, f32[8,512]{1,0:T(8,128)S(1)}, f32[8,512]{1,0:T(8,128)S(1)}, f32[64,8,512]{2,1,0:T(8,128)S(1)}, ...), condition=%wide.region_7.9_spmd.clone, body=%wide.region_5.8_spmd.clone.sunk | while | flops 1110019 | bytes 1302625 | solution.py:105
  67.2 0.6 tile.2
  67.8 3.3 %all-to-all-start.1 = ((f32[4,8,512]{2,1,0:T(8,128)}), f32[4,8,512]{2,1,0:T(8,128)S(1)}, u32[]{:S(2)}, u32[]{:S(2)}) async-start(f32[4,8,512]{2,1,0:T(8,128)} %tile.2), calls=%async_computation.1 | async-start | bytes 131072 | tf_op jit(solution)/shard_map/all_to_all | solution.py:129
  71.1 5.8 %all-to-all-done.1 = f32[4,8,512]{2,1,0:T(8,128)S(1)} async-done(((f32[4,8,512]{2,1,0:T(8,128)}), f32[4,8,512]{2,1,0:T(8,128)S(1)}, u32[]{:S(2)}, u32[]{:S(2)}) %all-to-all-start.1) | async-done | bytes 65568 | tf_op jit(solution)/shard_map/all_to_all | solution.py:129
  76.9 1.3 %collective-permute-start.4 = (f32[4,512]{1,0:T(4,128)S(1)}, f32[4,512]{1,0:T(4,128)S(1)}, u32[]{:S(2)}, u32[]{:S(2)}) collective-permute-start(f32[4,512]{1,0:T(4,128)S(1)} %get-tuple-element.136), channel_id=1, source_target_pairs={{2,0},{4,2},{6,4},{3,1},{5,3},{7,5},{10,8},{12,10},{14,12},{11,9},... | collective-permute-start | bytes 24584 | tf_op jit(solution)/shard_map/ppermute | solution.py:22
  78.2 3.2 %collective-permute-start.3 = (f32[4,512]{1,0:T(4,128)S(1)}, f32[4,512]{1,0:T(4,128)S(1)}, u32[]{:S(2)}, u32[]{:S(2)}) collective-permute-start(f32[4,512]{1,0:T(4,128)S(1)} %get-tuple-element.135), channel_id=1, source_target_pairs={{0,2},{2,4},{4,6},{1,3},{3,5},{5,7},{8,10},{10,12},{12,14},{9,11},... | collective-permute-start | bytes 24584 | tf_op jit(solution)/shard_map/ppermute | solution.py:21
  81.5 0.6 collective-permute-done.3
  82.1 1.5 %collective-permute-start.5 = (f32[4,40]{0,1:T(8,128)S(1)}, f32[4,40]{0,1:T(8,128)S(1)}, u32[]{:S(2)}, u32[]{:S(2)}) collective-permute-start(f32[4,40]{0,1:T(8,128)S(1)} %fusion.55), channel_id=1, source_target_pairs={{0,1},{1,0},{2,3},{3,2},{4,5},{5,4},{6,7},{7,6},{8,9},{9,8},{10,11... | collective-permute-start | bytes 1928 | tf_op jit(solution)/shard_map/ppermute | solution.py:41
  83.7 2.3 %collective-permute-done.5 = f32[4,40]{0,1:T(8,128)S(1)} collective-permute-done((f32[4,40]{0,1:T(8,128)S(1)}, f32[4,40]{0,1:T(8,128)S(1)}, u32[]{:S(2)}, u32[]{:S(2)}) %collective-permute-start.5) | collective-permute-done | bytes 672 | tf_op jit(solution)/shard_map/ppermute | solution.py:41
  86.1 0.6 multiply_add_fusion
  86.7 1.3 %fusion.45 = f32[8,32,512]{2,1,0:T(8,128)S(1)} fusion(f32[8,32,520]{2,1,0:T(8,128)S(1)} %multiply_add_fusion, f32[8]{0:T(128)S(1)} %get-tuple-element.142, f32[8]{0:T(128)S(1)} %get-tuple-element.143, f32[8]{0:T(128)S(1)} %get-tuple-element.144, f32[8]{0:T(128)S(1)} %get-tuple-element.145, f32[8]{0:T(128)S(1)} %get-tuple-element.146, ...), kind=kLoop, calls=%fused_computation.103 | loop fusion | flops 2228224 | bytes 5243168 | tf_op jit(solution)/shard_map/add | solution.py:144
  88.0 0.7 subtract_select_fusion
  88.7 1.6 %copy.44 = f32[16,32,512]{2,1,0:T(8,128)} copy(f32[16,32,512]{2,0,1:T(8,128)S(1)} %subtract_select_fusion) | data formatting | bytes 2097152
  90.3 0.6 copy.62
  (208 shorter events, 6.1 us)
Async XLA Ops:
  2.0 5.1 %copy-start.41 = (s32[16,2]{0,1:T(2,128)S(1)}, s32[16,2]{0,1:T(2,128)}, u32[]{:S(2)}) copy-start(s32[16,2]{0,1:T(2,128)} %param.11) | copy-start | bytes 388
  2.0 5.1 %copy-start.42 = (s32[16,2]{0,1:T(2,128)S(1)}, s32[16,2]{0,1:T(2,128)}, u32[]{:S(2)}) copy-start(s32[16,2]{0,1:T(2,128)} %param.10) | copy-start | bytes 388
  2.2 9.6 %copy-start = (f32[16,32,512]{2,1,0:T(8,128)S(1)}, f32[16,32,512]{2,1,0:T(8,128)}, u32[]{:S(2)}) copy-start(f32[16,32,512]{2,1,0:T(8,128)} %param.8) | copy-start | bytes 3145732
  2.2 8.5 %collective-permute-start = (f32[16,11,512]{2,0,1:T(8,128)S(1)}, f32[16,11,512]{2,0,1:T(8,128)}, u32[]{:S(2)}, u32[]{:S(2)}) collective-permute-start(f32[16,11,512]{2,0,1:T(8,128)S(1)} %copy.47), channel_id=1, source_target_pairs={{0,2},{2,4},{4,6},{1,3},{3,5},{5,7},{8,10},{10,12},{12,14},{9,11},... | collective-permute-start | bytes 1081352 | tf_op jit(solution)/shard_map/ppermute | solution.py:21
  5.7 6.7 %collective-permute-start.1 = (f32[16,11,512]{2,0,1:T(8,128)S(1)}, f32[16,11,512]{2,0,1:T(8,128)S(1)}, u32[]{:S(2)}, u32[]{:S(2)}) collective-permute-start(f32[16,11,512]{2,0,1:T(8,128)S(1)} %copy.48), channel_id=1, source_target_pairs={{2,0},{4,2},{6,4},{3,1},{5,3},{7,5},{10,8},{12,10},{14,12},{11,9},... | collective-permute-start | bytes 1081352 | tf_op jit(solution)/shard_map/ppermute | solution.py:22
  13.0 4.5 %collective-permute-start.2 = (f32[11,864]{1,0:T(8,128)S(1)}, f32[11,864]{1,0:T(8,128)S(1)}, u32[]{:S(2)}, u32[]{:S(2)}) collective-permute-start(f32[11,864]{1,0:T(8,128)S(1)} %reshape.187), channel_id=1, source_target_pairs={{0,1},{1,0},{2,3},{3,2},{4,5},{5,4},{6,7},{7,6},{8,9},{9,8},{10,11... | collective-permute-start | bytes 114056 | tf_op jit(solution)/shard_map/ppermute | solution.py:41
  18.4 1.0 %copy-start.19 = (f32[16]{0:T(128)S(1)}, f32[16]{0:T(128)}, u32[]{:S(2)}) copy-start(f32[16]{0:T(128)} %get-tuple-element.97) | copy-start | bytes 196
  18.4 1.0 %copy-start.20 = (f32[16]{0:T(128)S(1)}, f32[16]{0:T(128)}, u32[]{:S(2)}) copy-start(f32[16]{0:T(128)} %get-tuple-element.98) | copy-start | bytes 196
  19.6 4.0 %copy-start.1 = (s32[16,32,512]{2,1,0:T(8,128)S(1)}, s32[16,32,512]{2,1,0:T(8,128)}, u32[]{:S(2)}) copy-start(s32[16,32,512]{2,1,0:T(8,128)} %param.9) | copy-start | bytes 3145732
  19.6 4.0 %copy-start.2 = (f32[16]{0:T(128)S(1)}, f32[16]{0:T(128)}, u32[]{:S(2)}) copy-start(f32[16]{0:T(128)} %get-tuple-element.57) | copy-start | bytes 196
  19.6 4.0 %copy-start.3 = (f32[16]{0:T(128)S(1)}, f32[16]{0:T(128)}, u32[]{:S(2)}) copy-start(f32[16]{0:T(128)} %get-tuple-element.58) | copy-start | bytes 196
  19.6 4.0 %copy-start.4 = (f32[16]{0:T(128)S(1)}, f32[16]{0:T(128)}, u32[]{:S(2)}) copy-start(f32[16]{0:T(128)} %get-tuple-element.59) | copy-start | bytes 196
  19.6 4.0 %copy-start.5 = (f32[16]{0:T(128)S(1)}, f32[16]{0:T(128)}, u32[]{:S(2)}) copy-start(f32[16]{0:T(128)} %get-tuple-element.60) | copy-start | bytes 196
  19.6 4.0 %copy-start.6 = (f32[16]{0:T(128)S(1)}, f32[16]{0:T(128)}, u32[]{:S(2)}) copy-start(f32[16]{0:T(128)} %get-tuple-element.61) | copy-start | bytes 196
  19.6 4.0 %copy-start.7 = (f32[16]{0:T(128)S(1)}, f32[16]{0:T(128)}, u32[]{:S(2)}) copy-start(f32[16]{0:T(128)} %get-tuple-element.62) | copy-start | bytes 196
  19.7 4.0 %copy-start.8 = (f32[16]{0:T(128)S(1)}, f32[16]{0:T(128)}, u32[]{:S(2)}) copy-start(f32[16]{0:T(128)} %get-tuple-element.63) | copy-start | bytes 196
  19.7 4.0 %copy-start.9 = (f32[16]{0:T(128)S(1)}, f32[16]{0:T(128)}, u32[]{:S(2)}) copy-start(f32[16]{0:T(128)} %get-tuple-element.64) | copy-start | bytes 196
  19.7 4.0 %copy-start.10 = (f32[16]{0:T(128)S(1)}, f32[16]{0:T(128)}, u32[]{:S(2)}) copy-start(f32[16]{0:T(128)} %get-tuple-element.65) | copy-start | bytes 196
  19.7 4.0 %copy-start.11 = (f32[16]{0:T(128)S(1)}, f32[16]{0:T(128)}, u32[]{:S(2)}) copy-start(f32[16]{0:T(128)} %get-tuple-element.66) | copy-start | bytes 196
  19.7 4.0 %copy-start.12 = (f32[16]{0:T(128)S(1)}, f32[16]{0:T(128)}, u32[]{:S(2)}) copy-start(f32[16]{0:T(128)} %get-tuple-element.67) | copy-start | bytes 196
  19.7 4.0 %copy-start.13 = (f32[16]{0:T(128)S(1)}, f32[16]{0:T(128)}, u32[]{:S(2)}) copy-start(f32[16]{0:T(128)} %get-tuple-element.68) | copy-start | bytes 196
  19.7 4.0 %copy-start.14 = (f32[16]{0:T(128)S(1)}, f32[16]{0:T(128)}, u32[]{:S(2)}) copy-start(f32[16]{0:T(128)} %get-tuple-element.69) | copy-start | bytes 196
  19.7 4.0 %copy-start.15 = (f32[16]{0:T(128)S(1)}, f32[16]{0:T(128)}, u32[]{:S(2)}) copy-start(f32[16]{0:T(128)} %get-tuple-element.70) | copy-start | bytes 196
  19.7 4.0 %copy-start.16 = (f32[16]{0:T(128)S(1)}, f32[16]{0:T(128)}, u32[]{:S(2)}) copy-start(f32[16]{0:T(128)} %get-tuple-element.71) | copy-start | bytes 196
  19.7 4.0 %copy-start.17 = (f32[16]{0:T(128)S(1)}, f32[16]{0:T(128)}, u32[]{:S(2)}) copy-start(f32[16]{0:T(128)} %get-tuple-element.72) | copy-start | bytes 196
  19.8 4.0 %copy-start.18 = (f32[16]{0:T(128)S(1)}, f32[16]{0:T(128)}, u32[]{:S(2)}) copy-start(f32[16]{0:T(128)} %get-tuple-element.73) | copy-start | bytes 196
  30.8 31.8 %all-to-all-start = ((f32[16,32,512]{2,0,1:T(8,128)}), f32[16,32,512]{2,0,1:T(8,128)S(1)}, u32[]{:S(2)}, u32[]{:S(2)}) async-start(f32[16,32,512]{2,0,1:T(8,128)} %get-tuple-element.113), calls=%async_computation | async-start | bytes 2097152 | tf_op jit(solution)/shard_map/all_to_all | solution.py:127
  67.0 14.4 %copy-start.43 = (s32[16]{0:T(128)S(1)}, s32[16]{0:T(128)}, u32[]{:S(2)}) copy-start(s32[16]{0:T(128)} %param.12) | copy-start | bytes 196
  67.8 9.1 %all-to-all-start.1 = ((f32[4,8,512]{2,1,0:T(8,128)}), f32[4,8,512]{2,1,0:T(8,128)S(1)}, u32[]{:S(2)}, u32[]{:S(2)}) async-start(f32[4,8,512]{2,1,0:T(8,128)} %tile.2), calls=%async_computation.1 | async-start | bytes 131072 | tf_op jit(solution)/shard_map/all_to_all | solution.py:129
  76.9 4.5 %collective-permute-start.4 = (f32[4,512]{1,0:T(4,128)S(1)}, f32[4,512]{1,0:T(4,128)S(1)}, u32[]{:S(2)}, u32[]{:S(2)}) collective-permute-start(f32[4,512]{1,0:T(4,128)S(1)} %get-tuple-element.136), channel_id=1, source_target_pairs={{2,0},{4,2},{6,4},{3,1},{5,3},{7,5},{10,8},{12,10},{14,12},{11,9},... | collective-permute-start | bytes 24584 | tf_op jit(solution)/shard_map/ppermute | solution.py:22
  78.2 3.8 %collective-permute-start.3 = (f32[4,512]{1,0:T(4,128)S(1)}, f32[4,512]{1,0:T(4,128)S(1)}, u32[]{:S(2)}, u32[]{:S(2)}) collective-permute-start(f32[4,512]{1,0:T(4,128)S(1)} %get-tuple-element.135), channel_id=1, source_target_pairs={{0,2},{2,4},{4,6},{1,3},{3,5},{5,7},{8,10},{10,12},{12,14},{9,11},... | collective-permute-start | bytes 24584 | tf_op jit(solution)/shard_map/ppermute | solution.py:21
  82.1 3.8 %collective-permute-start.5 = (f32[4,40]{0,1:T(8,128)S(1)}, f32[4,40]{0,1:T(8,128)S(1)}, u32[]{:S(2)}, u32[]{:S(2)}) collective-permute-start(f32[4,40]{0,1:T(8,128)S(1)} %fusion.55), channel_id=1, source_target_pairs={{0,1},{1,0},{2,3},{3,2},{4,5},{5,4},{6,7},{7,6},{8,9},{9,8},{10,11... | collective-permute-start | bytes 1928 | tf_op jit(solution)/shard_map/ppermute | solution.py:41
  (20 other events, 19.5 us)
where the time goes:
time: 91.4 us; the launch traced here: 90.9 us
  waiting for transfers between devices  36.9 us (40%)
  starting transfers between devices  21.6 us (24%)
  other arithmetic  18.2 us (20%)
  local copies, waits for them, and re-layouts  11.5 us (13%)
  between operations  1.6 us (2%)
    all_to_all x1, waiting for transfers between devices, body(): lax.all_to_all(flagged, 'exp', split_axis=1, concat_axis=0, tiled=True)  26.2 us
    select_n x1, other arithmetic, body(): flagged = jnp.where(bad_pixels == 1, sentinel, warped)  6.99 us
    ppermute x2, starting transfers between devices, _row_halo(): lax.ppermute(lax.slice_in_dim(block, size - width, None, axis=dim), 'row'...  6.48 us
    all_to_all x1, waiting for transfers between devices, body(): lax.all_to_all(jnp.tile(band, (groups, 1)), 'exp', split_axis=0, concat_a...  5.8 us
    all_to_all x1, starting transfers between devices, body(): lax.all_to_all(flagged, 'exp', split_axis=1, concat_axis=0, tiled=True)  5.4 us
    unnamed x94, local copies, waits for them, and re-layouts  4.46 us
    ppermute x2, waiting for transfers between devices, _col_halo(): arrived = lax.ppermute(packed, 'col', [(0, 1), (1, 0)])  4.23 us
    ppermute x2, starting transfers between devices, _col_halo(): arrived = lax.ppermute(packed, 'col', [(0, 1), (1, 0)])  3.87 us
  transfers between devices with their start and end apart: 8, of which 5 were waited for; matrix products, arithmetic and copies ran while one was open for 7% of the time, Pallas kernels for 0%

commit v1 on v0

--- a/solution.py
+++ b/solution.py
@@ -11,6 +11,29 @@
 sentinel = 1000000.0
 half_sentinel = 500000.0
 pivot_span = 16.0
+
+
+def split_up(value, dim, size):
+    shape = value.shape
+    tiles = value.reshape(*shape[:dim], size, shape[dim] // size, *shape[dim + 1 :])
+    return jnp.moveaxis(tiles, dim, 0)
+
+
+def in_order(tiles, dim):
+    tiles = jnp.moveaxis(tiles, 0, dim)
+    dims = tiles.shape
+    return tiles.reshape(*dims[:dim], dims[dim] * dims[dim + 1], *dims[dim + 2 :])
+
+
+def exchange_in_pairs(array, axis, split_dim, concat_dim):
+    devices, index = (lax.axis_size(axis), lax.axis_index(axis))
+    tiles = split_up(array, split_dim, devices)
+    outs = [tiles[index]]
+    for step in range(1, devices):
+        sent = tiles[index ^ step]
+        outs.append(lax.ppermute(sent, axis, [(i, i ^ step) for i in range(devices)]))
+    tiles = jnp.stack(outs)[index ^ jnp.arange(devices)]
+    return in_order(tiles, concat_dim)
 
 
 def _row_halo(block, dim, width):
@@ -124,7 +147,7 @@
     across = resample_axis(padded, coef_down, row_count, 1)
     warped = resample_axis(across, coef_across, col_count, 2)
     flagged = jnp.where(bad_pixels == 1, sentinel, warped)
-    band = stack_median(lax.all_to_all(flagged, "exp", split_axis=1, concat_axis=0, tiled=True))
+    band = stack_median(exchange_in_pairs(flagged, "exp", 1, 0))
     groups = lax.axis_size("exp")
     median_sky = lax.all_to_all(
         jnp.tile(band, (groups, 1)), "exp", split_axis=0, concat_axis=0, tiled=True

time: 91.4 us -> 85.6 us (0.937)
  local copies, waits for them, and re-layouts: 11.5 us -> 6.85 us
  waiting for transfers between devices: 36.9 us -> 33.2 us
  other arithmetic: 18.2 us -> 21.7 us
    all_to_all x1 -> x0, waiting for transfers between devices: 26.2 us -> none  [body(): lax.all_to_all(flagged, 'exp', split_axis=1, concat_axis=0, tiled=True)]
    ppermute x0 -> x3, waiting for transfers between devices: none -> 22 us  [exchange_in_pairs(): lax.ppermute(sent, axis, [(i, i ^ step) for i in range(devices)])]
    reshape x0 -> x1, other arithmetic: none -> 7.57 us  [split_up(): value.reshape(*shape[:dim], size, shape[dim] // size, *shape[dim + 1:])]
    select_n x1, other arithmetic: 6.99 us -> 0.01 us  [exchange_in_pairs(): tiles = jnp.stack(outs)[index ^ jnp.arange(devices)]]
    all_to_all x1 -> x0, starting transfers between devices: 5.4 us -> none  [body(): lax.all_to_all(flagged, 'exp', split_axis=1, concat_axis=0, tiled=True)]
    ppermute x0 -> x3, starting transfers between devices: none -> 4.84 us  [exchange_in_pairs(): lax.ppermute(sent, axis, [(i, i ^ step) for i in range(devices)])]
    unnamed x94 -> x17, local copies, waits for them, and re-layouts: 4.46 us -> 1.44 us
    slice x4, local copies, waits for them, and re-layouts: 3.13 us -> 1.41 us  [resample_axis(): total = total + coefficients[:, position, None, None] * window]
  transfers between devices with their start and end apart: 8 -> 10, of which waited for: 5 -> 6; matrix products, arithmetic and copies ran while one was open for 7% -> 3% of each run, Pallas kernels for 0% -> 0%
where the time goes in v1:
time: 85.6 us; the launch traced here: 85.1 us
  waiting for transfers between devices  33.2 us (39%)
  other arithmetic  21.7 us (25%)
  starting transfers between devices  21.3 us (25%)
  local copies, waits for them, and re-layouts  6.85 us (8%)
  between operations  1 us (1%)
    ppermute x3, waiting for transfers between devices, exchange_in_pairs(): lax.ppermute(sent, axis, [(i, i ^ step) for i in range(devices)])  22 us
    reshape x1, other arithmetic, split_up(): value.reshape(*shape[:dim], size, shape[dim] // size, *shape[dim + 1:])  7.57 us
    ppermute x2, starting transfers between devices, _row_halo(): lax.ppermute(lax.slice_in_dim(block, size - width, None, axis=dim), 'row'...  6.27 us
    all_to_all x1, waiting for transfers between devices, body(): lax.all_to_all(jnp.tile(band, (groups, 1)), 'exp', split_axis=0, concat_a...  5.86 us
    ppermute x3, starting transfers between devices, exchange_in_pairs(): lax.ppermute(sent, axis, [(i, i ^ step) for i in range(devices)])  4.84 us
    ppermute x2, waiting for transfers between devices, _col_halo(): arrived = lax.ppermute(packed, 'col', [(0, 1), (1, 0)])  4.66 us
    ppermute x2, starting transfers between devices, _col_halo(): arrived = lax.ppermute(packed, 'col', [(0, 1), (1, 0)])  4.31 us
    add x1, other arithmetic, resample_axis(): total = total + coefficients[:, position, None, None] * window  4.15 us
  transfers between devices with their start and end apart: 10, of which 6 were waited for; matrix products, arithmetic and copies ran while one was open for 3% of the time, Pallas kernels for 0%

profile of v1, /device:TPU:0, one launch (start us, length us, event | category | flops | bytes accessed | tf_op | source)
XLA Modules:
  0.0 85.1 jit_solution(17753371791605788489)
XLA Ops:
  0.7 1.4 %fusion.136 = (f32[16,11,512]{2,1,0:T(8,128)S(1)}, f32[16,11,512]{2,1,0:T(8,128)S(1)}) fusion(f32[16,32,512]{2,1,0:T(8,128)} %param.8), kind=kLoop, calls=%fused_computation.323 | loop fusion | bytes 1441792 | tf_op jit(solution)/shard_map/slice | solution.py:44
  2.1 1.3 %collective-permute-start.1 = (f32[16,11,512]{2,1,0:T(8,128)S(1)}, f32[16,11,512]{2,1,0:T(8,128)S(1)}, u32[]{:S(2)}, u32[]{:S(2)}) collective-permute-start(f32[16,11,512]{2,1,0:T(8,128)S(1)} %get-tuple-element.115), channel_id=1, source_target_pairs={{2,0},{4,2},{6,4},{3,1},{5,3},{7,5},{10,8},{12,10},{14,12},{11,9},... | collective-permute-start | bytes 1081352 | tf_op jit(solution)/shard_map/ppermute | solution.py:45
  3.4 3.1 %collective-permute-start = (f32[16,11,512]{2,1,0:T(8,128)S(1)}, f32[16,11,512]{2,1,0:T(8,128)S(1)}, u32[]{:S(2)}, u32[]{:S(2)}) collective-permute-start(f32[16,11,512]{2,1,0:T(8,128)S(1)} %get-tuple-element.114), channel_id=1, source_target_pairs={{0,2},{2,4},{4,6},{1,3},{3,5},{5,7},{8,10},{10,12},{12,14},{9,11},... | collective-permute-start | bytes 1081352 | tf_op jit(solution)/shard_map/ppermute | solution.py:44
  7.8 0.5 slice_reduce_fusion.44
  8.3 0.5 slice_reduce_fusion.45
  9.4 3.0 %collective-permute-start.2 = (f32[11,864]{1,0:T(8,128)S(1)}, f32[11,864]{1,0:T(8,128)S(1)}, u32[]{:S(2)}, u32[]{:S(2)}) collective-permute-start(f32[11,864]{1,0:T(8,128)S(1)} %reshape.216), channel_id=1, source_target_pairs={{0,1},{1,0},{2,3},{3,2},{4,5},{5,4},{6,7},{7,6},{8,9},{9,8},{10,11... | collective-permute-start | bytes 114056 | tf_op jit(solution)/shard_map/ppermute | solution.py:64
  12.5 2.2 %collective-permute-done.2 = f32[11,864]{1,0:T(8,128)S(1)} collective-permute-done((f32[11,864]{1,0:T(8,128)S(1)}, f32[11,864]{1,0:T(8,128)S(1)}, u32[]{:S(2)}, u32[]{:S(2)}) %collective-permute-start.2) | collective-permute-done | bytes 38048 | tf_op jit(solution)/shard_map/ppermute | solution.py:64
  14.7 0.3 copy.19
  15.1 0.3 copy.18
  15.4 1.0 %pad_maximum_fusion = f32[16,54,534]{2,1,0:T(8,128)S(1)} fusion(f32[16,54,11]{2,1,0:T(8,128)S(1)} %copy.19, f32[16,11,512]{2,1,0:T(8,128)S(1)} %collective-permute-done.1, f32[16,32,512]{2,1,0:T(8,128)S(1)} %copy-done, f32[16,11,512]{2,1,0:T(8,128)S(1)} %collective-permute-done, f32[16,54,11]{2,1,0:T(8,128)S(1)} %copy.18), kind=kLoop, calls=%fused_computation.7 | loop fusion | flops 1845504 | bytes 3691008 | tf_op jit(solution)/shard_map/concatenate | solution.py:69
  16.5 4.1 %fusion = f32[16,32,534]{2,1,0:T(8,128)S(1)} fusion(f32[16,54,534]{2,1,0:T(8,128)S(1)} %pad_maximum_fusion, f32[16]{0:T(128)S(1)} %get-tuple-element.73, f32[16]{0:T(128)S(1)} %get-tuple-element.74, f32[16]{0:T(128)S(1)} %get-tuple-element.75, f32[16]{0:T(128)S(1)} %get-tuple-element.76, f32[16]{0:T(128)S(1)} %get-tuple-element.77, ...), kind=kLoop, calls=%fused_computation.9 | loop fusion | flops 12303360 | bytes 26248640 | tf_op jit(solution)/shard_map/add | solution.py:112
  20.6 7.6 %select_bitcast_fusion = (f32[16,4,8,512]{3,2,1,0:T(8,128)S(1)}, f32[16,32,512]{2,1,0:T(8,128)S(1)}, pred[16,32,512]{2,1,0:T(8,128)(4,1)S(1)}) fusion(f32[16,32,534]{2,1,0:T(8,128)S(1)} %fusion, f32[16]{0:T(128)S(1)} %get-tuple-element.50, f32[16]{0:T(128)S(1)} %get-tuple-element.51, f32[16]{0:T(128)S(1)} %get-tuple-element.52, ...), kind=kLoop, calls=%fused_computation.102 | loop fusion | flops 12320768 | bytes 27526592 | tf_op jit(solution)/shard_map/reshape | solution.py:18
  28.3 4.2 %collective-permute-start.5 = (f32[16,8,512]{2,1,0:T(8,128)S(1)}, f32[16,8,512]{2,1,0:T(8,128)S(1)}, u32[]{:S(2)}, u32[]{:S(2)}) collective-permute-start(f32[16,8,512]{2,1,0:T(8,128)S(1)} %get-tuple-element.111), channel_id=1, source_target_pairs={{0,24},{8,16},{16,8},{24,0},{1,25},{9,17},{17,9},{25,1},{2,26},{10... | collective-permute-start | bytes 786440 | tf_op jit(solution)/shard_map/ppermute | solution.py:34
  32.5 0.6 collective-permute-start.3
  33.2 3.8 %collective-permute-done.5 = f32[16,8,512]{2,1,0:T(8,128)S(1)} collective-permute-done((f32[16,8,512]{2,1,0:T(8,128)S(1)}, f32[16,8,512]{2,1,0:T(8,128)S(1)}, u32[]{:S(2)}, u32[]{:S(2)}) %collective-permute-start.5) | collective-permute-done | bytes 262176 | tf_op jit(solution)/shard_map/ppermute | solution.py:34
  37.0 18.2 %collective-permute-done.4 = f32[16,8,512]{2,1,0:T(8,128)S(1)} collective-permute-done((f32[16,8,512]{2,1,0:T(8,128)S(1)}, f32[16,8,512]{2,1,0:T(8,128)S(1)}, u32[]{:S(2)}, u32[]{:S(2)}) %collective-permute-start.4) | collective-permute-done | bytes 262176 | tf_op jit(solution)/shard_map/ppermute | solution.py:34
  55.3 0.7 copy-done.3
  56.1 1.2 %pad_maximum_fusion.1 = f32[4,16,8,512]{3,2,1,0:T(8,128)S(1)} fusion(f32[1,16,8,512]{3,2,1,0:T(8,128)} %bitcast.93, f32[1,16,8,512]{3,2,1,0:T(8,128)} %bitcast.94, f32[1,16,8,512]{3,2,1,0:T(8,128)} %bitcast.95, f32[1,16,8,512]{3,2,1,0:T(8,128)S(1)} %get-tuple-element.110), kind=kLoop, calls=%fused_computation.99 | loop fusion | flops 786432 | bytes 2097152 | tf_op jit(solution)/shard_map/stack | solution.py:35
  57.2 0.6 gather_fusion
  58.0 3.6 %while.13 = (s32[]{:T(128)}, f32[8,512]{1,0:T(8,128)S(1)}, f32[8,512]{1,0:T(8,128)S(1)}, f32[64,8,512]{2,1,0:T(8,128)S(1)}, f32[8,512]{1,0:T(8,128)S(1)}, /*index=5*/s32[]{:T(128)}, s32[]{:T(128)}) while((s32[]{:T(128)}, f32[8,512]{1,0:T(8,128)S(1)}, f32[8,512]{1,0:T(8,128)S(1)}, f32[64,8,512]{2,1,0:T(8,128)S(1)}, ...), condition=%wide.region_7.9_spmd.clone, body=%wide.region_5.8_spmd.clone.sunk | while | flops 1110019 | bytes 1302625 | solution.py:128
  61.8 0.6 tile.2
  62.4 3.3 %all-to-all-start = ((f32[4,8,512]{2,1,0:T(8,128)}), f32[4,8,512]{2,1,0:T(8,128)S(1)}, u32[]{:S(2)}, u32[]{:S(2)}) async-start(f32[4,8,512]{2,1,0:T(8,128)} %tile.2), calls=%async_computation | async-start | bytes 131072 | tf_op jit(solution)/shard_map/all_to_all | solution.py:152
  65.7 5.9 %all-to-all-done = f32[4,8,512]{2,1,0:T(8,128)S(1)} async-done(((f32[4,8,512]{2,1,0:T(8,128)}), f32[4,8,512]{2,1,0:T(8,128)S(1)}, u32[]{:S(2)}, u32[]{:S(2)}) %all-to-all-start) | async-done | bytes 65568 | tf_op jit(solution)/shard_map/all_to_all | solution.py:152
  71.6 1.3 %collective-permute-start.7 = (f32[4,512]{1,0:T(4,128)S(1)}, f32[4,512]{1,0:T(4,128)S(1)}, u32[]{:S(2)}, u32[]{:S(2)}) collective-permute-start(f32[4,512]{1,0:T(4,128)S(1)} %get-tuple-element.134), channel_id=1, source_target_pairs={{2,0},{4,2},{6,4},{3,1},{5,3},{7,5},{10,8},{12,10},{14,12},{11,9},... | collective-permute-start | bytes 24584 | tf_op jit(solution)/shard_map/ppermute | solution.py:45
  72.9 3.2 %collective-permute-start.6 = (f32[4,512]{1,0:T(4,128)S(1)}, f32[4,512]{1,0:T(4,128)S(1)}, u32[]{:S(2)}, u32[]{:S(2)}) collective-permute-start(f32[4,512]{1,0:T(4,128)S(1)} %get-tuple-element.133), channel_id=1, source_target_pairs={{0,2},{2,4},{4,6},{1,3},{3,5},{5,7},{8,10},{10,12},{12,14},{9,11},... | collective-permute-start | bytes 24584 | tf_op jit(solution)/shard_map/ppermute | solution.py:44
  76.1 0.6 collective-permute-done.6
  76.8 1.3 %collective-permute-start.8 = (f32[4,40]{0,1:T(8,128)S(1)}, f32[4,40]{0,1:T(8,128)S(1)}, u32[]{:S(2)}, u32[]{:S(2)}) collective-permute-start(f32[4,40]{0,1:T(8,128)S(1)} %fusion.56), channel_id=1, source_target_pairs={{0,1},{1,0},{2,3},{3,2},{4,5},{5,4},{6,7},{7,6},{8,9},{9,8},{10,11... | collective-permute-start | bytes 1928 | tf_op jit(solution)/shard_map/ppermute | solution.py:64
  78.1 2.5 %collective-permute-done.8 = f32[4,40]{0,1:T(8,128)S(1)} collective-permute-done((f32[4,40]{0,1:T(8,128)S(1)}, f32[4,40]{0,1:T(8,128)S(1)}, u32[]{:S(2)}, u32[]{:S(2)}) %collective-permute-start.8) | collective-permute-done | bytes 672 | tf_op jit(solution)/shard_map/ppermute | solution.py:64
  80.8 0.6 multiply_add_fusion
  81.4 1.3 %fusion.45 = f32[8,32,512]{2,1,0:T(8,128)S(1)} fusion(f32[8,32,520]{2,1,0:T(8,128)S(1)} %multiply_add_fusion, f32[8]{0:T(128)S(1)} %get-tuple-element.140, f32[8]{0:T(128)S(1)} %get-tuple-element.141, f32[8]{0:T(128)S(1)} %get-tuple-element.142, f32[8]{0:T(128)S(1)} %get-tuple-element.143, f32[8]{0:T(128)S(1)} %get-tuple-element.144, ...), kind=kLoop, calls=%fused_computation.105 | loop fusion | flops 2228224 | bytes 5243168 | tf_op jit(solution)/shard_map/add | solution.py:167
  82.7 1.8 %subtract_select_fusion = f32[16,32,512]{2,1,0:T(8,128)} fusion(pred[16,32,512]{2,1,0:T(8,128)(4,1)S(1)} %get-tuple-element.109, f32[16,32,512]{2,1,0:T(8,128)S(1)} %get-tuple-element.108, f32[32,512]{1,0:T(8,128)S(1)} %get-tuple-element.117, f32[16]{0:T(128)S(1)} %get-tuple-element.149, f32[32,512]{1,0:T(8,128)S(1)} %get-tuple-element.118, ...), kind=kLoop, calls=%fused_computation.100 | loop fusion | flops 4456448 | bytes 2884096 | tf_op jit(solution)/shard_map/jit(_where)/select_n | solution.py:175
  84.5 0.6 copy.30
  (138 shorter events, 5.9 us)
Async XLA Ops:
  0.6 8.2 %copy-start = (f32[16,32,512]{2,1,0:T(8,128)S(1)}, f32[16,32,512]{2,1,0:T(8,128)}, u32[]{:S(2)}) copy-start(f32[16,32,512]{2,1,0:T(8,128)} %param.8) | copy-start | bytes 3145732
  0.6 5.8 %copy-start.5 = (s32[16,2]{0,1:T(2,128)S(1)}, s32[16,2]{0,1:T(2,128)}, u32[]{:S(2)}) copy-start(s32[16,2]{0,1:T(2,128)} %param.11) | copy-start | bytes 388
  0.7 5.9 %copy-start.6 = (s32[16,2]{0,1:T(2,128)S(1)}, s32[16,2]{0,1:T(2,128)}, u32[]{:S(2)}) copy-start(s32[16,2]{0,1:T(2,128)} %param.10) | copy-start | bytes 388
  2.1 6.8 %collective-permute-start.1 = (f32[16,11,512]{2,1,0:T(8,128)S(1)}, f32[16,11,512]{2,1,0:T(8,128)S(1)}, u32[]{:S(2)}, u32[]{:S(2)}) collective-permute-start(f32[16,11,512]{2,1,0:T(8,128)S(1)} %get-tuple-element.115), channel_id=1, source_target_pairs={{2,0},{4,2},{6,4},{3,1},{5,3},{7,5},{10,8},{12,10},{14,12},{11,9},... | collective-permute-start | bytes 1081352 | tf_op jit(solution)/shard_map/ppermute | solution.py:45
  3.4 5.5 %collective-permute-start = (f32[16,11,512]{2,1,0:T(8,128)S(1)}, f32[16,11,512]{2,1,0:T(8,128)S(1)}, u32[]{:S(2)}, u32[]{:S(2)}) collective-permute-start(f32[16,11,512]{2,1,0:T(8,128)S(1)} %get-tuple-element.114), channel_id=1, source_target_pairs={{0,2},{2,4},{4,6},{1,3},{3,5},{5,7},{8,10},{10,12},{12,14},{9,11},... | collective-permute-start | bytes 1081352 | tf_op jit(solution)/shard_map/ppermute | solution.py:44
  9.4 5.2 %collective-permute-start.2 = (f32[11,864]{1,0:T(8,128)S(1)}, f32[11,864]{1,0:T(8,128)S(1)}, u32[]{:S(2)}, u32[]{:S(2)}) collective-permute-start(f32[11,864]{1,0:T(8,128)S(1)} %reshape.216), channel_id=1, source_target_pairs={{0,1},{1,0},{2,3},{3,2},{4,5},{5,4},{6,7},{7,6},{8,9},{9,8},{10,11... | collective-permute-start | bytes 114056 | tf_op jit(solution)/shard_map/ppermute | solution.py:64
  16.4 4.2 %copy-start.1 = (s32[16,32,512]{2,1,0:T(8,128)S(1)}, s32[16,32,512]{2,1,0:T(8,128)}, u32[]{:S(2)}) copy-start(s32[16,32,512]{2,1,0:T(8,128)} %param.9) | copy-start | bytes 3145732
  28.3 8.7 %collective-permute-start.5 = (f32[16,8,512]{2,1,0:T(8,128)S(1)}, f32[16,8,512]{2,1,0:T(8,128)S(1)}, u32[]{:S(2)}, u32[]{:S(2)}) collective-permute-start(f32[16,8,512]{2,1,0:T(8,128)S(1)} %get-tuple-element.111), channel_id=1, source_target_pairs={{0,24},{8,16},{16,8},{24,0},{1,25},{9,17},{17,9},{25,1},{2,26},{10... | collective-permute-start | bytes 786440 | tf_op jit(solution)/shard_map/ppermute | solution.py:34
  32.5 22.8 %collective-permute-start.4 = (f32[16,8,512]{2,1,0:T(8,128)S(1)}, f32[16,8,512]{2,1,0:T(8,128)S(1)}, u32[]{:S(2)}, u32[]{:S(2)}) collective-permute-start(f32[16,8,512]{2,1,0:T(8,128)S(1)} %get-tuple-element.112), channel_id=1, source_target_pairs={{0,16},{8,24},{16,0},{24,8},{1,17},{9,25},{17,1},{25,9},{2,18},{10... | collective-permute-start | bytes 786440 | tf_op jit(solution)/shard_map/ppermute | solution.py:34
  32.5 22.8 %collective-permute-start.3 = (f32[16,8,512]{2,1,0:T(8,128)S(1)}, f32[16,8,512]{2,1,0:T(8,128)S(1)}, u32[]{:S(2)}, u32[]{:S(2)}) collective-permute-start(f32[16,8,512]{2,1,0:T(8,128)S(1)} %get-tuple-element.113), channel_id=1, source_target_pairs={{0,8},{8,0},{16,24},{24,16},{1,9},{9,1},{17,25},{25,17},{2,10},{10... | collective-permute-start | bytes 786440 | tf_op jit(solution)/shard_map/ppermute | solution.py:34
  37.0 18.2 %copy-start.2 = (f32[16,8,512]{2,1,0:T(8,128)}, f32[16,8,512]{2,1,0:T(8,128)S(1)}, u32[]{:S(2)}) copy-start(f32[16,8,512]{2,1,0:T(8,128)S(1)} %collective-permute-done.5) | copy-start | bytes 786436
  55.3 0.7 copy-start.3
  55.3 0.8 copy-start.4
  61.6 14.5 %copy-start.7 = (s32[16]{0:T(128)S(1)}, s32[16]{0:T(128)}, u32[]{:S(2)}) copy-start(s32[16]{0:T(128)} %param.12) | copy-start | bytes 196
  62.4 9.2 %all-to-all-start = ((f32[4,8,512]{2,1,0:T(8,128)}), f32[4,8,512]{2,1,0:T(8,128)S(1)}, u32[]{:S(2)}, u32[]{:S(2)}) async-start(f32[4,8,512]{2,1,0:T(8,128)} %tile.2), calls=%async_computation | async-start | bytes 131072 | tf_op jit(solution)/shard_map/all_to_all | solution.py:152
  71.6 4.5 %collective-permute-start.7 = (f32[4,512]{1,0:T(4,128)S(1)}, f32[4,512]{1,0:T(4,128)S(1)}, u32[]{:S(2)}, u32[]{:S(2)}) collective-permute-start(f32[4,512]{1,0:T(4,128)S(1)} %get-tuple-element.134), channel_id=1, source_target_pairs={{2,0},{4,2},{6,4},{3,1},{5,3},{7,5},{10,8},{12,10},{14,12},{11,9},... | collective-permute-start | bytes 24584 | tf_op jit(solution)/shard_map/ppermute | solution.py:45
  72.9 3.8 %collective-permute-start.6 = (f32[4,512]{1,0:T(4,128)S(1)}, f32[4,512]{1,0:T(4,128)S(1)}, u32[]{:S(2)}, u32[]{:S(2)}) collective-permute-start(f32[4,512]{1,0:T(4,128)S(1)} %get-tuple-element.133), channel_id=1, source_target_pairs={{0,2},{2,4},{4,6},{1,3},{3,5},{5,7},{8,10},{10,12},{12,14},{9,11},... | collective-permute-start | bytes 24584 | tf_op jit(solution)/shard_map/ppermute | solution.py:44
  76.8 3.8 %collective-permute-start.8 = (f32[4,40]{0,1:T(8,128)S(1)}, f32[4,40]{0,1:T(8,128)S(1)}, u32[]{:S(2)}, u32[]{:S(2)}) collective-permute-start(f32[4,40]{0,1:T(8,128)S(1)} %fusion.56), channel_id=1, source_target_pairs={{0,1},{1,0},{2,3},{3,2},{4,5},{5,4},{6,7},{7,6},{8,9},{9,8},{10,11... | collective-permute-start | bytes 1928 | tf_op jit(solution)/shard_map/ppermute | solution.py:64
